TPU v7x, 512 devices: a whole 4x4x16 slice. The times are simulated.
512 devices in a mesh: clip: 16 (over y, z_hi), seq: 32 (over x, z_lo, core).
Axes of the slice: x: 4, y: 4, z: 16 (z_hi: 4, z_lo: 4; z = z_hi * 4 + z_lo), core: 2. Of those that a mesh axis runs over, the one named last changes fastest.
Arguments:
- frames_in: bfloat16 [512, 256, 1152], P(('clip', 'seq')), parts along dimension 0, may hold values from -6 to 6
- modulation: float32 [48, 1152], P('clip'), parts along dimension 0, may hold values from -3 to 3
- self_proj: bfloat16 [1152, 1728], P(None, 'seq'), may hold values from -0.1875 to 0.1875
- self_out: bfloat16 [576, 1152], P(None, 'seq'), may hold values from -0.25 to 0.25
- cross_query: bfloat16 [1152, 576], P(None, 'seq'), may hold values from -0.1875 to 0.1875
- cross_keyval: bfloat16 [1152, 1152], P(None, 'seq'), may hold values from -0.1875 to 0.1875
- cross_out: bfloat16 [576, 1152], P(None, 'seq'), may hold values from -0.25 to 0.25
- text_bank: bfloat16 [32, 256, 1152], P('seq'), may hold values from -6 to 6
- prompt_pick: int32 [16], P('clip'), parts along dimension 0, may hold values from 0 to 31
- text_lengths: int32 [32], replicated, may hold values from 32 to 256
Outputs:
- frames_out: bfloat16 [512, 256, 1152], P(('clip', 'seq')), parts along dimension 0
There are 16 independent parts, one for each index of `clip`. A program takes and returns all parts, laid end to end along the dimension named above; an argument that names none is the same for every part. Nothing has to cross between parts.
All inputs are finite; a program needn't handle non-finite values.
Results may differ from a plain program's by a relative error of at most 0.006.
Values may be sent and summed in bfloat16 or wider, within the bound.
No kernel may reach another device: no remote copies, remote signals or barrier semaphores. Data moves between devices by JAX's collectives and lax.ppermute only.
A program may use at most 64 MiB of HBM per device.

v0:
```python
import math
import jax
import jax.numpy as jnp
from jax import lax
from jax.sharding import PartitionSpec as P

HEAD_DIM = 72
EPS = 1e-06


def spread_2(block, axis, owner):
    block = jnp.where(lax.axis_index(axis) == owner, block, jnp.zeros_like(block))
    return lax.psum(block, axis)


def layer_norm(values):
    mean = jnp.mean(values, axis=-1, keepdims=True)
    centred = values - mean
    spread = jnp.mean(centred * centred, axis=-1, keepdims=True)
    return centred * lax.rsqrt(spread + EPS)


def head_norm(values, heads):
    shaped = values.reshape(values.shape[:-1] + (heads, values.shape[-1] // heads))
    power = jnp.mean(shaped * shaped, axis=-1, keepdims=True)
    return shaped * lax.rsqrt(power + EPS)


def temporal_attention(qkv, heads, attn, scale_q):
    frames, patches = (qkv.shape[0], qkv.shape[1])
    query = (head_norm(qkv[..., :attn].astype(jnp.float32), heads) * scale_q).astype(jnp.bfloat16)
    key = head_norm(qkv[..., attn : 2 * attn].astype(jnp.float32), heads).astype(jnp.bfloat16)
    value = qkv[..., 2 * attn :].reshape(frames, patches, heads, attn // heads)
    scores = jnp.einsum("fphd,gphd->phfg", query, key, preferred_element_type=jnp.float32)
    weights = jnp.exp(scores)
    total = jnp.sum(weights, axis=-1)
    probs = weights.astype(jnp.bfloat16)
    mixed = jnp.einsum("phfg,gphd->fphd", probs, value, preferred_element_type=jnp.float32)
    attended = mixed / jnp.transpose(total, (2, 0, 1))[..., None]
    return attended.astype(jnp.bfloat16).reshape(frames, patches, attn)


def per_device(
    frames_in,
    modulation,
    self_proj,
    self_out,
    cross_query,
    cross_keyval,
    cross_out,
    text_bank,
    prompt_pick,
    text_lengths,
):
    count = lax.axis_size("seq")
    frame_rows, pixels, width = frames_in.shape
    attn = self_out.shape[0]
    heads = attn // HEAD_DIM
    scale_q = 1.0 / math.sqrt(HEAD_DIM)
    pix_dev = pixels // count
    frames = frame_rows * count
    tokens = frames_in.astype(jnp.float32)
    normed = (layer_norm(tokens) * (1.0 + modulation[1]) + modulation[0]).astype(jnp.bfloat16)
    switched = lax.all_to_all(normed, "seq", split_axis=1, concat_axis=0, tiled=True)
    flat_pix = switched.reshape(-1, width)
    qkv = jnp.dot(
        flat_pix,
        lax.all_gather(self_proj, "seq", axis=1, tiled=True),
        preferred_element_type=jnp.float32,
    ).astype(jnp.bfloat16)
    qkv = qkv.reshape(frames, pix_dev, 3 * attn)
    out_self, query_weight, out_cross = (
        lax.all_gather(self_out, "seq", axis=1, tiled=True),
        lax.all_gather(cross_query, "seq", axis=1, tiled=True),
        lax.all_gather(cross_out, "seq", axis=1, tiled=True),
    )
    attended = temporal_attention(qkv, heads, attn, scale_q)
    returned = lax.all_to_all(attended, "seq", split_axis=0, concat_axis=1, tiled=True)
    self_term = jnp.dot(returned.reshape(-1, attn), out_self, preferred_element_type=jnp.float32)
    after_self = (tokens.reshape(-1, width) + modulation[2] * self_term).astype(jnp.bfloat16)
    pick = prompt_pick[0]
    memory = spread_2(text_bank[0], "seq", pick)
    own_columns = jnp.dot(memory, cross_keyval, preferred_element_type=jnp.float32).astype(
        jnp.bfloat16
    )
    keyval = lax.all_gather(own_columns, "seq", axis=1, tiled=True)
    text_len = keyval.shape[0]
    text_key = head_norm(keyval[:, :attn].astype(jnp.float32), heads).astype(jnp.bfloat16)
    text_value = keyval[:, attn:].reshape(text_len, heads, HEAD_DIM)
    slots = jnp.arange(text_lengths.shape[0], dtype=jnp.int32)
    length = jnp.sum(jnp.where(slots == pick, text_lengths, 0))
    live = jnp.arange(text_len, dtype=jnp.int32) < length
    text_query = jnp.dot(after_self, query_weight, preferred_element_type=jnp.float32)
    text_query = (head_norm(text_query, heads) * scale_q).astype(jnp.bfloat16)
    cross_scores = jnp.einsum(
        "thd,lhd->thl", text_query, text_key, preferred_element_type=jnp.float32
    )
    cross_weights = jnp.where(live, jnp.exp(cross_scores), 0.0)
    cross_total = jnp.sum(cross_weights, axis=-1)
    cross_probs = cross_weights.astype(jnp.bfloat16)
    cross_mix = jnp.einsum(
        "thl,lhd->thd", cross_probs, text_value, preferred_element_type=jnp.float32
    )
    crossed = (cross_mix / cross_total[..., None]).astype(jnp.bfloat16).reshape(-1, attn)
    cross_term = jnp.dot(crossed, out_cross, preferred_element_type=jnp.float32)
    frames_out = (after_self.astype(jnp.float32) + cross_term).astype(jnp.bfloat16)
    return frames_out.reshape(frame_rows, pixels, width)


def solution(mesh):
    placed = (
        P(("clip", "seq"), None, None),
        P("clip", None),
        P(None, "seq"),
        P(None, "seq"),
        P(None, "seq"),
        P(None, "seq"),
        P(None, "seq"),
        P("seq", None, None),
        P("clip"),
        P(),
    )
    return jax.shard_map(
        per_device,
        mesh=mesh,
        in_specs=placed,
        out_specs=P(("clip", "seq"), None, None),
        check_vma=False,
    )
```

profile of v0, /device:TPU:1, one launch (start us, length us, event | category | flops | bytes accessed | tf_op | source)
XLA Modules:
  0.0 582.2 jit_solution(11461628995922027875)
XLA Ops:
  11.0 0.9 copy.54
  12.5 4.3 reduce.8
  16.9 1.0 reshape.164
  17.9 10.4 %all-to-all-start = ((bf16[32,2,4608]{2,1,0:T(2,128)(2,1)}), bf16[32,2,4608]{2,1,0:T(2,128)(2,1)S(1)}, u32[]{:S(2)}, u32[]{:S(2)}) async-start(bf16[32,2,4608]{2,1,0:T(2,128)(2,1)} %reshape.164), calls=%async_computation | async-start | bytes 1179648 | tf_op jit(solution)/shard_map/all_to_all | solution.py:64
  29.6 20.2 %all-to-all-done = bf16[32,2,4608]{2,1,0:T(2,128)(2,1)S(1)} async-done(((bf16[32,2,4608]{2,1,0:T(2,128)(2,1)}), bf16[32,2,4608]{2,1,0:T(2,128)(2,1)S(1)}, u32[]{:S(2)}, u32[]{:S(2)}) %all-to-all-start) | async-done | bytes 589856 | tf_op jit(solution)/shard_map/all_to_all | solution.py:64
  50.2 37.1 %all-gather.10.cloned.1.call-done = bf16[32,54,1152]{2,1,0:T(8,128)(2,1)} async-done(((bf16[1,54,1152]{2,1,0:T(8,128)(2,1)}), bf16[32,54,1152]{2,1,0:T(8,128)(2,1)}) %all-gather.10.cloned.1.call-update) | async-done | bytes 3981328 | tf_op jit(solution)/shard_map/all_gather | solution.py:68
  87.3 5.0 reshape.150
  92.3 3.5 convolution_convert_fusion
  97.8 1.0 multiply_reduce_fusion
  99.3 1.6 reshape.130
  102.0 0.9 fusion.35
  103.9 1.1 reshape.135
  104.9 6.6 %all-to-all-start.1 = ((bf16[32,8,576]{2,1,0:T(8,128)(2,1)}), bf16[32,8,576]{2,1,0:T(8,128)(2,1)}, u32[]{:S(2)}, u32[]{:S(2)}) async-start(bf16[32,8,576]{2,1,0:T(8,128)(2,1)} %reshape.135), calls=%async_computation.1 | async-start | bytes 655360 | tf_op jit(solution)/shard_map/all_to_all | solution.py:78
  112.2 254.0 %all-reduce.2.cloned.1.call-done = bf16[256,1152]{1,0:T(8,128)(2,1)} async-done(((bf16[256,1152]{1,0:T(8,128)(2,1)}), bf16[256,1152]{1,0:T(8,128)(2,1)}) %all-reduce.2.cloned.1.call-update) | async-done | bytes 589840 | tf_op jit(solution)/shard_map/psum | solution.py:13
  366.1 1.4 fusion.14
  367.5 44.5 %all-gather.2 = bf16[32,36,256]{2,1,0:T(8,128)(2,1)S(1)} all-gather(bf16[1,36,256]{2,1,0:T(8,128)(2,1)S(1)} %fusion.14), channel_id=1, replica_groups=mesh['clip'=16,'seq'=32] {'seq'}, dimensions={0}, use_global_device_ids=true | all-gather | bytes 608256 | tf_op jit(solution)/shard_map/all_gather | solution.py:86
  413.7 21.1 %all-gather.12.cloned.1.call-done = bf16[32,36,576]{2,1,0:T(8,128)(2,1)} async-done(((bf16[1,36,576]{2,1,0:T(8,128)(2,1)}), bf16[32,36,576]{2,1,0:T(8,128)(2,1)}) %all-gather.12.cloned.1.call-update) | async-done | bytes 1327120 | tf_op jit(solution)/shard_map/all_gather | solution.py:73
  434.8 3.5 reshape.152
  438.3 62.6 %all-gather.14.cloned.1.call-done = bf16[32,18,1152]{2,1,0:T(8,128)(2,1)} async-done(((bf16[1,18,1152]{2,1,0:T(8,128)(2,1)}), bf16[32,18,1152]{2,1,0:T(8,128)(2,1)}) %all-gather.14.cloned.1.call-update) | async-done | bytes 1327120 | tf_op jit(solution)/shard_map/all_gather | solution.py:74
  500.9 2.4 reshape.156
  503.3 63.6 %all-gather.16.cloned.1.call-done = bf16[32,36,576]{2,1,0:T(8,128)(2,1)} async-done(((bf16[1,36,576]{2,1,0:T(8,128)(2,1)}), bf16[32,36,576]{2,1,0:T(8,128)(2,1)}) %all-gather.16.cloned.1.call-update) | async-done | bytes 1327120 | tf_op jit(solution)/shard_map/all_gather | solution.py:75
  567.0 2.5 reshape.158
  569.5 2.2 fusion.2
  574.1 1.5 fusion.3
  (57 shorter events, 15.1 us)
Async XLA Ops:
  6.5 359.6 %copy-start = (bf16[1152,36]{0,1:T(8,128)(2,1)S(1)}, bf16[1152,36]{0,1:T(8,128)(2,1)}, u32[]{:S(2)}) copy-start(bf16[1152,36]{0,1:T(8,128)(2,1)} %param.15) | copy-start | bytes 248836
  6.5 3.6 copy-start.6
  6.5 3.7 copy-start.1
  6.5 80.8 %all-gather.10.cloned.1.call-start = ((), (), s32[]{:S(2)}) async-start(), calls=%async_computation.3 | async-start | bytes 4257792 | tf_op jit(solution)/shard_map/all_gather | solution.py:68
  7.3 358.8 %all-reduce.2.cloned.1.call-start = ((), (), s32[]{:S(2)}) async-start(), calls=%async_computation.2 | async-start | bytes 1179648 | tf_op jit(solution)/shard_map/psum | solution.py:13
  8.9 425.9 %all-gather.12.cloned.1.call-start = ((), (), s32[]{:S(2)}) async-start(), calls=%async_computation.4 | async-start | bytes 1689600 | tf_op jit(solution)/shard_map/all_gather | solution.py:73
  9.6 491.3 %all-gather.14.cloned.1.call-start = ((), (), s32[]{:S(2)}) async-start(), calls=%async_computation.5 | async-start | bytes 1824768 | tf_op jit(solution)/shard_map/all_gather | solution.py:74
  16.9 12.1 %copy-start.7 = (s32[32]{0:T(128)S(1)}, s32[32]{0:T(128)}, u32[]{:S(2)}) copy-start(s32[32]{0:T(128)} %param.19) | copy-start | bytes 388
  17.9 31.8 %all-to-all-start = ((bf16[32,2,4608]{2,1,0:T(2,128)(2,1)}), bf16[32,2,4608]{2,1,0:T(2,128)(2,1)S(1)}, u32[]{:S(2)}, u32[]{:S(2)}) async-start(bf16[32,2,4608]{2,1,0:T(2,128)(2,1)} %reshape.164), calls=%async_computation | async-start | bytes 1179648 | tf_op jit(solution)/shard_map/all_to_all | solution.py:64
  28.4 538.6 %all-gather.16.cloned.1.call-start = ((), (), s32[]{:S(2)}) async-start(), calls=%async_computation.6 | async-start | bytes 1689600 | tf_op jit(solution)/shard_map/all_gather | solution.py:75
  99.3 1.9 copy-start.4
  104.9 464.5 %all-to-all-start.1 = ((bf16[32,8,576]{2,1,0:T(8,128)(2,1)}), bf16[32,8,576]{2,1,0:T(8,128)(2,1)}, u32[]{:S(2)}, u32[]{:S(2)}) async-start(bf16[32,8,576]{2,1,0:T(8,128)(2,1)} %reshape.135), calls=%async_computation.1 | async-start | bytes 655360 | tf_op jit(solution)/shard_map/all_to_all | solution.py:78
  412.8 0.8 copy-start.2
  571.7 1.0 copy-start.3
  572.6 1.0 copy-start.5
Sparse Core Ops, SparseCore 0:
  9.5 77.7 all-gather.9
  90.3 275.7 all-reduce.1
  368.5 66.2 all-gather.11
  437.0 63.8 all-gather.13
  503.1 63.7 all-gather.15
where the time goes:
time: 583 us; the launch traced here: 582 us
  waiting for transfers between devices  461 us (79%)
  blocking collectives  44.5 us (8%)
  local copies, waits for them, and re-layouts  23.2 us (4%)
  starting transfers between devices  17.4 us (3%)
  between operations  14.1 us (2%)
  matrix products  11.8 us (2%)
  other arithmetic  10.3 us (2%)
    psum x1, waiting for transfers between devices, spread_2(): return lax.psum(block, axis)  254 us
    all_gather x1, waiting for transfers between devices, per_device(): lax.all_gather(cross_out, 'seq', axis=1, tiled=True)  63.6 us
    all_gather x1, waiting for transfers between devices, per_device(): lax.all_gather(cross_query, 'seq', axis=1, tiled=True)  62.6 us
    all_gather x1, blocking collectives, per_device(): keyval = lax.all_gather(own_columns, 'seq', axis=1, tiled=True)  44.5 us
    all_gather x1, waiting for transfers between devices, per_device(): lax.all_gather(self_proj, 'seq', axis=1, tiled=True)  37.1 us
    all_gather x1, waiting for transfers between devices, per_device(): lax.all_gather(self_out, 'seq', axis=1, tiled=True)  21.1 us
    all_to_all x1, waiting for transfers between devices, per_device(): lax.all_to_all(normed, 'seq', split_axis=1, concat_axis=0, tiled=True)  20.2 us
    unnamed x24, local copies, waits for them, and re-layouts  17.1 us
  transfers between devices with their start and end apart: 7, of which 6 were waited for; matrix products, arithmetic and copies ran while one was open for 7% of the time, Pallas kernels for 0%

commit v1 on v0

--- a/solution.py
+++ b/solution.py
@@ -10,7 +10,7 @@
 
 def spread_2(block, axis, owner):
     block = jnp.where(lax.axis_index(axis) == owner, block, jnp.zeros_like(block))
-    return lax.psum(block, axis)
+    return jnp.sum(lax.all_gather(block, axis), axis=0)
 
 
 def layer_norm(values):

time: 583 us -> 471 us (0.81)
  waiting for transfers between devices: 461 us -> 324 us
  blocking collectives: 44.5 us -> 75.9 us
  starting transfers between devices: 17.4 us -> 5.75 us
  other arithmetic: 10.3 us -> 19.1 us
    psum x1 -> x0, waiting for transfers between devices: 254 us -> none  [spread_2(): return lax.psum(block, axis)]
    all_gather x0 -> x1, waiting for transfers between devices: none -> 111 us  [spread_2(): return jnp.sum(lax.all_gather(block, axis), axis=0)]
    all_to_all x0 -> x1, blocking collectives: none -> 30.7 us  [per_device(): lax.all_to_all(normed, 'seq', split_axis=1, concat_axis=0, tiled=True)]
    all_gather x1, waiting for transfers between devices: 21.1 us -> 45.4 us  [per_device(): lax.all_gather(self_out, 'seq', axis=1, tiled=True)]
    all_to_all x1 -> x0, waiting for transfers between devices: 20.2 us -> none  [per_device(): lax.all_to_all(normed, 'seq', split_axis=1, concat_axis=0, tiled=True)]
    all_to_all x1 -> x0, starting transfers between devices: 10.4 us -> none  [per_device(): lax.all_to_all(normed, 'seq', split_axis=1, concat_axis=0, tiled=True)]
    reduce_sum x0 -> x1, other arithmetic: none -> 9.95 us  [spread_2(): return jnp.sum(lax.all_gather(block, axis), axis=0)]
    unnamed x24 -> x22, local copies, waits for them, and re-layouts: 17.1 us -> 15.8 us
  transfers between devices with their start and end apart: 7 -> 6, of which waited for: 6 -> 5; matrix products, arithmetic and copies ran while one was open for 7% -> 8% of each run, Pallas kernels for 0% -> 0%
where the time goes in v1:
time: 471 us; the launch traced here: 470 us
  waiting for transfers between devices  324 us (69%)
  blocking collectives  75.9 us (16%)
  local copies, waits for them, and re-layouts  21 us (4%)
  other arithmetic  19.1 us (4%)
  between operations  14.1 us (3%)
  matrix products  10.7 us (2%)
  starting transfers between devices  5.75 us (1%)
    all_gather x1, waiting for transfers between devices, spread_2(): return jnp.sum(lax.all_gather(block, axis), axis=0)  111 us
    all_gather x1, waiting for transfers between devices, per_device(): lax.all_gather(cross_out, 'seq', axis=1, tiled=True)  63.4 us
    all_gather x1, waiting for transfers between devices, per_device(): lax.all_gather(cross_query, 'seq', axis=1, tiled=True)  63 us
    all_gather x1, waiting for transfers between devices, per_device(): lax.all_gather(self_out, 'seq', axis=1, tiled=True)  45.4 us
    all_gather x1, blocking collectives, per_device(): keyval = lax.all_gather(own_columns, 'seq', axis=1, tiled=True)  45.2 us
    all_gather x1, waiting for transfers between devices, per_device(): lax.all_gather(self_proj, 'seq', axis=1, tiled=True)  38.3 us
    all_to_all x1, blocking collectives, per_device(): lax.all_to_all(normed, 'seq', split_axis=1, concat_axis=0, tiled=True)  30.7 us
    unnamed x22, local copies, waits for them, and re-layouts  15.8 us
  transfers between devices with their start and end apart: 6, of which 5 were waited for; matrix products, arithmetic and copies ran while one was open for 8% of the time, Pallas kernels for 0%

profile of v1, /device:TPU:1, one launch (start us, length us, event | category | flops | bytes accessed | tf_op | source)
XLA Modules:
  0.0 470.1 jit_solution(7402782862727938438)
XLA Ops:
  6.5 0.7 all-gather.13.cloned.1.call-update
  10.0 0.9 broadcast_select_fusion
  11.8 0.9 copy.54
  13.3 4.4 reduce.9
  17.9 30.7 %all_to_all.8 = bf16[32,2,4608]{2,1,0:T(2,128)(2,1)S(1)} all-to-all(bf16[32,2,4608]{2,1,0:T(2,128)(2,1)S(1)} %reshape.161), channel_id=1, replica_groups=mesh['clip'=16,'seq'=32] {'seq'}, dimensions={0} | all-to-all | bytes 1179648 | tf_op jit(solution)/shard_map/all_to_all | solution.py:64
  49.1 38.3 %all-gather.13.cloned.1.call-done = bf16[32,54,1152]{2,1,0:T(8,128)(2,1)} async-done(((bf16[1,54,1152]{2,1,0:T(8,128)(2,1)}), bf16[32,54,1152]{2,1,0:T(8,128)(2,1)}) %all-gather.13.cloned.1.call-update) | async-done | bytes 3981328 | tf_op jit(solution)/shard_map/all_gather | solution.py:68
  87.4 5.1 %reshape.147 = bf16[1728,1152]{1,0:T(8,128)(2,1)} reshape(bf16[32,54,1152]{2,1,0:T(8,128)(2,1)} %all-gather.13.cloned.1.call-done) | data formatting | bytes 7962624
  92.4 3.5 convolution_convert_fusion
  96.7 1.3 reshape.127
  99.8 0.7 multiply_convert_fusion
  100.5 0.9 fusion.35
  102.5 1.1 reshape.132
  103.6 5.6 %all-to-all-start.1 = ((bf16[32,8,576]{2,1,0:T(8,128)(2,1)}), bf16[32,8,576]{2,1,0:T(8,128)(2,1)}, u32[]{:S(2)}, u32[]{:S(2)}) async-start(bf16[32,8,576]{2,1,0:T(8,128)(2,1)} %reshape.132), calls=%async_computation.1 | async-start | bytes 655360 | tf_op jit(solution)/shard_map/all_to_all | solution.py:78
  110.5 45.4 %all-gather.15.cloned.1.call-done = bf16[32,36,576]{2,1,0:T(8,128)(2,1)} async-done(((bf16[1,36,576]{2,1,0:T(8,128)(2,1)}), bf16[32,36,576]{2,1,0:T(8,128)(2,1)}) %all-gather.15.cloned.1.call-update) | async-done | bytes 1327120 | tf_op jit(solution)/shard_map/all_gather | solution.py:73
  155.9 3.5 reshape.149
  159.4 63.0 %all-gather.17.cloned.1.call-done = bf16[32,18,1152]{2,1,0:T(8,128)(2,1)} async-done(((bf16[1,18,1152]{2,1,0:T(8,128)(2,1)}), bf16[32,18,1152]{2,1,0:T(8,128)(2,1)}) %all-gather.17.cloned.1.call-update) | async-done | bytes 1327120 | tf_op jit(solution)/shard_map/all_gather | solution.py:74
  222.4 2.4 reshape.153
  224.8 63.4 %all-gather.19.cloned.1.call-done = bf16[32,36,576]{2,1,0:T(8,128)(2,1)} async-done(((bf16[1,36,576]{2,1,0:T(8,128)(2,1)}), bf16[32,36,576]{2,1,0:T(8,128)(2,1)}) %all-gather.19.cloned.1.call-update) | async-done | bytes 1327120 | tf_op jit(solution)/shard_map/all_gather | solution.py:75
  288.3 2.5 reshape.155
  290.8 2.2 fusion.2
  293.8 110.9 %all-gather.11.cloned.1.call-done = bf16[32,256,1152]{2,1,0:T(8,128)(2,1)} async-done(((bf16[1,256,1152]{2,1,0:T(8,128)(2,1)}), bf16[32,256,1152]{2,1,0:T(8,128)(2,1)}) %all-gather.11.cloned.1.call-update) | async-done | bytes 18874384 | tf_op jit(solution)/shard_map/all_gather | solution.py:13
  404.7 10.0 %reduce_sum.98 = bf16[256,1152]{1,0:T(8,128)(2,1)S(1)} reduce(bf16[32,256,1152]{2,1,0:T(8,128)(2,1)} %all-gather.11.cloned.1.call-done, bf16[]{:T(256)} %constant.29.clone.1), dimensions={0}, to_apply=%region_5.6 | reduce | flops 9142272 | bytes 19464194 | tf_op jit(solution)/shard_map/reduce_sum | solution.py:13
  415.0 45.2 %all-gather.2 = bf16[32,36,256]{2,1,0:T(8,128)(2,1)S(1)} all-gather(bf16[1,36,256]{2,1,0:T(8,128)(2,1)S(1)} %fusion.14), channel_id=1, replica_groups=mesh['clip'=16,'seq'=32] {'seq'}, dimensions={0}, use_global_device_ids=true | all-gather | bytes 608256 | tf_op jit(solution)/shard_map/all_gather | solution.py:86
  462.1 1.5 fusion.3
  (55 shorter events, 12.0 us)
Async XLA Ops:
  6.5 408.1 %copy-start = (bf16[1152,36]{0,1:T(8,128)(2,1)S(1)}, bf16[1152,36]{0,1:T(8,128)(2,1)}, u32[]{:S(2)}) copy-start(bf16[1152,36]{0,1:T(8,128)(2,1)} %param.15) | copy-start | bytes 248836
  6.5 4.4 copy-start.5
  6.5 4.4 copy-start.1
  6.5 80.8 %all-gather.13.cloned.1.call-start = ((), (), s32[]{:S(2)}) async-start(), calls=%async_computation.3 | async-start | bytes 4257792 | tf_op jit(solution)/shard_map/all_gather | solution.py:68
  7.3 148.6 %all-gather.15.cloned.1.call-start = ((), (), s32[]{:S(2)}) async-start(), calls=%async_computation.4 | async-start | bytes 1689600 | tf_op jit(solution)/shard_map/all_gather | solution.py:73
  8.0 214.4 %all-gather.17.cloned.1.call-start = ((), (), s32[]{:S(2)}) async-start(), calls=%async_computation.5 | async-start | bytes 1824768 | tf_op jit(solution)/shard_map/all_gather | solution.py:74
  8.7 279.5 %all-gather.19.cloned.1.call-start = ((), (), s32[]{:S(2)}) async-start(), calls=%async_computation.6 | async-start | bytes 1689600 | tf_op jit(solution)/shard_map/all_gather | solution.py:75
  9.3 395.4 %all-gather.11.cloned.1.call-start = ((), (), s32[]{:S(2)}) async-start(), calls=%async_computation.2 | async-start | bytes 19464192 | tf_op jit(solution)/shard_map/all_gather | solution.py:13
  100.5 1.0 copy-start.4
  102.3 6.9 %copy-start.6 = (s32[32]{0:T(128)S(1)}, s32[32]{0:T(128)}, u32[]{:S(2)}) copy-start(s32[32]{0:T(128)} %param.19) | copy-start | bytes 388
  103.6 187.2 %all-to-all-start.1 = ((bf16[32,8,576]{2,1,0:T(8,128)(2,1)}), bf16[32,8,576]{2,1,0:T(8,128)(2,1)}, u32[]{:S(2)}, u32[]{:S(2)}) async-start(bf16[32,8,576]{2,1,0:T(8,128)(2,1)} %reshape.132), calls=%async_computation.1 | async-start | bytes 655360 | tf_op jit(solution)/shard_map/all_to_all | solution.py:78
  293.0 0.8 copy-start.2
  461.0 1.1 copy-start.3
Sparse Core Ops, SparseCore 0:
  9.5 77.8 all-gather.12
  89.5 66.3 all-gather.14
  158.1 64.3 all-gather.16
  224.4 63.7 all-gather.18
  290.3 114.4 all-gather.10
